TPU v7x, 128 devices: a whole 4x4x4 slice. The times are simulated.
128 devices in a mesh: ctl: 32 (over y, z_lo, x), side: 2 (over core), tp: 2 (over z_hi).
Axes of the slice: x: 4, y: 4, z: 4 (z_hi: 2, z_lo: 2; z = z_hi * 2 + z_lo), core: 2. Of those that a mesh axis runs over, the one named last changes fastest.
Arguments:
- image_latent: bfloat16 [64, 256, 3072], P('ctl'), may hold values from -6 to 6
- control_latent: bfloat16 [64, 256, 3072], P('ctl'), may hold values from -6 to 6
- control_order: int32 [64, 256], P('ctl'), may hold values from 0 to 255, each once within a row
- captions: bfloat16 [128, 128, 3072], P('ctl'), may hold values from -6 to 6
- caption_ids: int32 [64], P('ctl'), may hold values from 0 to 3
- modulation: float32 [2, 64, 3, 3072], P('side', 'ctl'), may hold values from -3 to 3
- qkv_weight: bfloat16 [2, 3072, 3, 1536], P('side', 'ctl', None, 'tp'), may hold values from -1 to 1
- qk_gain: float32 [2, 2, 128], P('side'), may hold values from 1 to 6
- out_weight: bfloat16 [2, 1536, 3072], P('side', 'tp', 'ctl'), may hold values from -0.5 to 0.5
- zero_weight: bfloat16 [3072, 3072], P('ctl', 'tp'), may hold values from -0.109375 to 0.109375
- proj_weight: bfloat16 [3072, 64], P('tp'), may hold values from -1 to 1
- final_mod: float32 [64, 2, 3072], P('ctl'), may hold values from -3 to 3
- velocity_target: float32 [64, 256, 64], P('ctl'), may hold values from -6 to 6
Outputs:
- hidden_out: bfloat16 [2, 64, 256, 3072], P('side', 'ctl', None, 'tp')
- zero_grad: float32 [3072, 3072], P(('ctl', 'side'), 'tp')
Inputs may be any that keep to these rules, and one draw needn't show every extreme that they name: caption_ids counts from the first caption held by the sample's own index of ctl. Each sample's row of control_order is a permutation.
All inputs are finite; a program needn't handle non-finite values.
Results may differ from a plain program's by a relative error of at most 0.03.
Values may be sent and summed in bfloat16 or wider, within the bound.
No kernel may reach another device: no remote copies, remote signals or barrier semaphores. Data moves between devices by JAX's collectives and lax.ppermute only.
A program may use at most 192 MiB of HBM per device.

v0:
```python
import math
import jax
import jax.numpy as jnp
from jax import lax
from jax.sharding import PartitionSpec as P

HEAD_DIM = 128
EPS = 1e-06


def passed_along(shard, axis, by):
    length = lax.axis_size(axis)
    pairs = [(i, i + by) for i in range(length) if 0 <= i + by < length]
    return lax.ppermute(shard, axis, pairs)


def partner(value, axis, bit):
    mask = 2**bit
    pairs = [(source, source ^ mask) for source in range(lax.axis_size(axis))]
    return lax.ppermute(value, axis, pairs)


def swap(value, axis):
    return lax.ppermute(value, axis, [(0, 1), (1, 0)])


def layer_norm(values):
    center = values - jnp.mean(values, axis=-1, keepdims=True)
    spread = jnp.mean(center * center, axis=-1, keepdims=True)
    return center * lax.rsqrt(spread + EPS)


def head_norm(values, gain_row):
    power_mean = jnp.mean(values * values, axis=-1, keepdims=True)
    return (values * lax.rsqrt(power_mean + EPS) * gain_row).astype(jnp.bfloat16)


def rounded(values):
    narrow = lax.optimization_barrier(values.astype(jnp.bfloat16))
    return narrow.astype(jnp.float32)


def local(
    image_latent,
    control_latent,
    control_order,
    captions,
    caption_ids,
    modulation,
    qkv_weight,
    qk_gain,
    out_weight,
    zero_weight,
    proj_weight,
    final_mod,
    velocity_target,
):
    side_index = lax.axis_index("side")
    tp_index = lax.axis_index("tp")
    ctl_count = lax.axis_size("ctl")
    tp_count = lax.axis_size("tp")
    is_control = side_index == 0
    micro_count, img_rows, width_full = image_latent.shape
    text_rows = captions.shape[1]
    seq_rows = text_rows + img_rows
    local_heads = qkv_weight.shape[3]
    head_count = local_heads // HEAD_DIM
    half_width = width_full // tp_count
    quarter_width = half_width // 2
    flat_rows = micro_count * img_rows
    block_rows = width_full // (2 * ctl_count)
    aligned = jax.vmap(lambda latent, order_row: jnp.take(latent, order_row, axis=0))(
        control_latent, control_order
    )
    plain_rows = image_latent.astype(jnp.float32)
    hidden = plain_rows + jnp.where(is_control, 1.0, 0.0) * aligned.astype(jnp.float32)
    chosen = jnp.take(captions, caption_ids, axis=0).astype(jnp.float32)
    sequence = jnp.concatenate([chosen, hidden], axis=1)
    modulate = modulation[0]
    normed = (layer_norm(sequence) * (1.0 + modulate[:, 1:2]) + modulate[:, 0:1]).astype(
        jnp.bfloat16
    )
    text_flat = normed.reshape(micro_count * seq_rows, width_full)
    image_flat = normed[:, text_rows:].reshape(flat_rows, width_full)
    local_rows = qkv_weight.shape[1]
    own_cols = lax.dynamic_slice_in_dim(zero_weight, side_index * quarter_width, quarter_width, 1)
    packed = jnp.concatenate(
        [qkv_weight[0].reshape(local_rows, 3 * local_heads), out_weight[0].T, own_cols], axis=1
    )
    gathered = lax.all_gather(packed, "ctl", axis=0, tiled=True)
    count_rows = gathered.shape[0]
    query_weight = gathered[:, :local_heads]
    pair_weight = gathered[:, local_heads : 3 * local_heads]
    out_cols = gathered[:, 3 * local_heads : 4 * local_heads]
    zero_cols = gathered[:, 4 * local_heads :]
    query_acc = jnp.dot(image_flat, query_weight, preferred_element_type=jnp.float32)
    pair_acc = jnp.dot(text_flat, pair_weight, preferred_element_type=jnp.float32)
    gain_pair = qk_gain[0]
    queries = head_norm(
        query_acc.reshape(micro_count, img_rows, head_count, HEAD_DIM), gain_pair[0]
    )
    pair_acc = pair_acc.reshape(micro_count, seq_rows, 2, head_count, HEAD_DIM)
    keys_all = head_norm(pair_acc[:, :, 0], gain_pair[1])
    values_all = pair_acc[:, :, 1].astype(jnp.bfloat16)
    scores = jnp.einsum(
        "bihd,bjhd->bhij", queries, keys_all, preferred_element_type=jnp.float32
    ) / math.sqrt(HEAD_DIM)
    attend = jax.nn.softmax(scores, axis=-1).astype(jnp.bfloat16)
    mixed_heads = jnp.einsum(
        "bhij,bjhd->bihd", attend, values_all, preferred_element_type=jnp.float32
    )
    mixed_heads = mixed_heads.astype(jnp.bfloat16).reshape(flat_rows, local_heads)
    contract_last = (((1,), (1,)), ((), ()))
    other_out = lax.dynamic_slice_in_dim(out_cols, (1 - tp_index) * half_width, half_width, 0)
    own_out = lax.dynamic_slice_in_dim(out_cols, tp_index * half_width, half_width, 0)
    other_part = lax.dot_general(
        mixed_heads, other_out, contract_last, preferred_element_type=jnp.float32
    ).astype(jnp.bfloat16)
    got_part = swap(other_part, "tp")
    own_part_heads = rounded(
        lax.dot_general(mixed_heads, own_out, contract_last, preferred_element_type=jnp.float32)
    )
    head_sum = own_part_heads + got_part.astype(jnp.float32)
    hid_half = lax.dynamic_slice_in_dim(hidden, tp_index * half_width, half_width, 2)
    gate_half = lax.dynamic_slice_in_dim(modulate[:, 2:3], tp_index * half_width, half_width, 2)
    act_half = hid_half + gate_half * head_sum.reshape(micro_count, img_rows, half_width)
    act_half = act_half.reshape(flat_rows, half_width)
    act_own = act_half.astype(jnp.bfloat16)
    act_got = swap(act_own, "tp")
    act_narrow = jnp.where(
        tp_index == 0,
        jnp.concatenate([act_own, act_got], axis=1),
        jnp.concatenate([act_got, act_own], axis=1),
    )
    act_other = passed_along(act_narrow, "side", 1)
    control_rows = jnp.where(is_control, act_narrow, act_other)
    own_part = jnp.dot(control_rows, zero_cols, preferred_element_type=jnp.float32)
    own_narrow = own_part.astype(jnp.bfloat16)
    other_narrow = partner(own_narrow, "side", 0)
    residual_narrow = jnp.where(
        is_control,
        jnp.concatenate([own_narrow, other_narrow], axis=1),
        jnp.concatenate([other_narrow, own_narrow], axis=1),
    )
    merged = act_half + residual_narrow.astype(jnp.float32)
    section_out = jnp.where(is_control, residual_narrow, merged.astype(jnp.bfloat16))
    final_half = lax.dynamic_slice_in_dim(final_mod, tp_index * half_width, half_width, 2)
    merged_rows = merged.reshape(micro_count, img_rows, half_width)
    row_total, squares = lax.psum(
        (
            jnp.sum(merged_rows, axis=-1, keepdims=True),
            jnp.sum(merged_rows * merged_rows, axis=-1, keepdims=True),
        ),
        "tp",
    )
    mean_val = row_total / width_full
    spread = squares / width_full - mean_val * mean_val
    scale_inv = lax.rsqrt(spread + EPS)
    unit_rows = (merged_rows - mean_val) * scale_inv
    final_in = (unit_rows * (1.0 + final_half[:, 1:2]) + final_half[:, 0:1]).astype(jnp.bfloat16)
    pred_part = jnp.dot(
        final_in.reshape(flat_rows, half_width), proj_weight, preferred_element_type=jnp.float32
    )
    prediction = pred_part + swap(pred_part, "tp")
    loss_factor = 4.0 / math.sqrt(micro_count * ctl_count * img_rows)
    grad_pred = (loss_factor * (prediction - velocity_target.reshape(flat_rows, -1))).astype(
        jnp.bfloat16
    )
    grad_unit = lax.dot_general(
        grad_pred, proj_weight, (((1,), (1,)), ((), ())), preferred_element_type=jnp.float32
    )
    grad_unit = grad_unit.reshape(micro_count, img_rows, half_width) * (1.0 + final_half[:, 1:2])
    first_sum, second_sum = lax.psum(
        (
            jnp.sum(grad_unit, axis=-1, keepdims=True),
            jnp.sum(grad_unit * unit_rows, axis=-1, keepdims=True),
        ),
        "tp",
    )
    grad_narrow = (
        (grad_unit - first_sum / width_full - unit_rows * (second_sum / width_full)) * scale_inv
    ).astype(jnp.bfloat16)
    grad_narrow = grad_narrow.reshape(flat_rows, half_width)
    returned = passed_along(grad_narrow, "side", -1)
    grad_rows_all = jnp.where(is_control, returned, grad_narrow)
    own_act = lax.dynamic_index_in_dim(
        control_rows.reshape(flat_rows, ctl_count, 2, block_rows), side_index, 2, keepdims=False
    )
    own_act = own_act.reshape(flat_rows, ctl_count * block_rows)
    product = lax.dot_general(
        own_act, grad_rows_all, (((0,), (0,)), ((), ())), preferred_element_type=jnp.float32
    )
    group_parts = rounded(product).astype(jnp.bfloat16).reshape(ctl_count, block_rows, half_width)
    received = lax.all_to_all(group_parts, "ctl", 0, 0, tiled=True)
    zero_grad = jnp.sum(received.astype(jnp.float32), axis=0)
    return (section_out.reshape(1, micro_count, img_rows, half_width), zero_grad)


def solution(mesh):
    return jax.shard_map(
        local,
        mesh=mesh,
        in_specs=(
            P("ctl", None, None),
            P("ctl", None, None),
            P("ctl", None),
            P("ctl", None, None),
            P("ctl"),
            P("side", "ctl", None, None),
            P("side", "ctl", None, "tp"),
            P("side", None, None),
            P("side", "tp", "ctl"),
            P("ctl", "tp"),
            P("tp", None),
            P("ctl", None, None),
            P("ctl", None, None),
        ),
        out_specs=(P("side", "ctl", None, "tp"), P(("ctl", "side"), "tp")),
        check_vma=False,
    )
```

profile of v0, /device:TPU:113, one launch (start us, length us, event | category | flops | bytes accessed | tf_op | source)
XLA Modules:
  0.0 585.1 jit_solution(12119574096527699242)
XLA Ops:
  12.6 14.8 %gather_fusion.1 = bf16[512,3072]{1,0:T(8,128)(2,1)} fusion(bf16[2,256,3072]{2,1,0:T(8,128)(2,1)S(1)} %copy-done, s32[512]{0:T(512)S(1)} %bitcast.109), kind=kCustom, calls=%fused_computation.1 | custom fusion | bytes 6295552 | tf_op jit(solution)/shard_map/vmap(jit(_take))/gather | solution.py:72
  27.4 3.7 gather_fusion
  32.9 4.4 multiply_add_fusion
  40.0 3.6 add_convert_fusion
  43.6 228.4 %all-gather.2.cloned.1.call-done = bf16[3072,3840]{1,0:T(8,128)(2,1)} async-done(((bf16[96,3840]{1,0:T(8,128)(2,1)}), bf16[3072,3840]{1,0:T(8,128)(2,1)}) %all-gather.2.cloned.1.call-update) | async-done | bytes 23592976 | tf_op jit(solution)/shard_map/all_gather | solution.py:90
  272.0 8.0 %slice_bitcast_fusion = bf16[1536,3072]{0,1:T(8,128)(2,1)} fusion(bf16[3072,3840]{1,0:T(8,128)(2,1)} %all-gather.2.cloned.1.call-done), kind=kLoop, calls=%fused_computation.3 | loop fusion | bytes 18874368 | tf_op jit(solution)/shard_map/dot_general | solution.py:97
  280.0 12.6 %copy.21 = bf16[1536,3072]{1,0:T(8,128)(2,1)} copy(bf16[1536,3072]{0,1:T(8,128)(2,1)} %slice_bitcast_fusion) | data formatting | bytes 18874368 | tf_op jit(solution)/shard_map/dot_general | solution.py:97
  292.7 11.5 %fusion.4 = f32[2,384,2,6,128]{1,4,3,2,0:T(8,128)S(1)} fusion(bf16[2,6,128,3072,1]{3,2,1,0,4:T(8,128)(2,1)} %bitcast.113, bf16[2,384,3072]{2,1,0:T(8,128)(2,1)} %add_convert_fusion), kind=kOutput, calls=%fused_computation.14 | convolution fusion | flops 7247757312 | bytes 18874368 | tf_op jit(solution)/shard_map/dot_general | solution.py:97
  306.6 8.2 %fusion.46 = (bf16[3072,768]{1,0:T(8,128)(2,1)}, bf16[768,3072]{0,1:T(8,128)(2,1)}) fusion(bf16[3072,3840]{1,0:T(8,128)(2,1)} %all-gather.2.cloned.1.call-done), kind=kLoop, calls=%fused_computation.99 | loop fusion | bytes 18874368 | tf_op jit(solution)/shard_map/slice | solution.py:94
  314.7 6.7 %copy.22 = bf16[768,3072]{1,0:T(8,128)(2,1)} copy(bf16[768,3072]{0,1:T(8,128)(2,1)} %get-tuple-element.10) | data formatting | bytes 9437184 | tf_op jit(solution)/shard_map/dot_general | solution.py:96
  321.4 6.0 %multiply_reduce_fusion.5 = (f32[2,256,6]{1,2,0:T(8,128)S(1)}, f32[2,256,6,128]{1,3,2,0:T(8,128)S(1)}) fusion(bf16[6,128,3072,1]{2,1,0,3:T(8,128)(2,1)} %bitcast.118, bf16[2,384,3072]{2,1,0:T(8,128)(2,1)} %add_convert_fusion), kind=kOutput, calls=%fused_computation.48 | convolution fusion | flops 2416702464 | bytes 9449472 | tf_op jit(solution)/shard_map/dot_general | solution.py:96
  327.4 2.6 fusion.22
  333.9 10.0 %fusion.21 = bf16[2,256,6,128]{1,3,2,0:T(8,128)(2,1)S(1)} fusion(f32[2,6,256]{2,1,0:T(8,128)S(1)} %fusion.48, f32[2,384,2,6,128]{1,4,3,2,0:T(8,128)} %copy-done.9, f32[2,6,256,384]{3,2,1,0:T(8,128)} %copy-done.4), kind=kOutput, calls=%fused_computation.53 | convolution fusion | flops 308284800 | bytes 11415552 | tf_op jit(solution)/shard_map/bhij,bjhd->bihd/dot_general | solution.py:109
  344.9 3.1 convolution_convert_fusion.1
  349.0 3.1 convolution_convert_fusion.2
  352.1 32.9 %collective-permute-done = bf16[512,1536]{1,0:T(8,128)(2,1)} collective-permute-done((bf16[512,1536]{1,0:T(8,128)(2,1)S(1)}, bf16[512,1536]{1,0:T(8,128)(2,1)}, u32[]{:S(2)}, u32[]{:S(2)}) %collective-permute-start) | collective-permute-done | bytes 1572896 | tf_op jit(solution)/shard_map/ppermute | solution.py:24
  386.8 4.9 fusion.27
  394.6 34.8 %collective-permute-done.1 = bf16[512,1536]{0,1:T(8,128)(2,1)} collective-permute-done((bf16[512,1536]{0,1:T(8,128)(2,1)S(1)}, bf16[512,1536]{0,1:T(8,128)(2,1)}, u32[]{:S(2)}, u32[]{:S(2)}) %collective-permute-start.1) | collective-permute-done | bytes 1572896 | tf_op jit(solution)/shard_map/ppermute | solution.py:24
  429.4 3.2 maximum_select_fusion
  433.9 7.7 %collective-permute-done.2 = bf16[512,3072]{0,1:T(8,128)(2,1)S(1)} collective-permute-done((bf16[512,3072]{0,1:T(8,128)(2,1)S(1)}, bf16[512,3072]{0,1:T(8,128)(2,1)S(1)}, u32[]{:S(2)}, u32[]{:S(2)}) %collective-permute-start.2) | collective-permute-done | bytes 3145760 | tf_op jit(solution)/shard_map/ppermute | solution.py:14
  442.0 6.1 %fusion.18 = bf16[512,768]{1,0:T(8,128)(2,1)S(1)} fusion(bf16[512,3072]{0,1:T(8,128)(2,1)S(1)} %broadcast_select_fusion, bf16[3072,3840]{1,0:T(8,128)(2,1)} %all-gather.2.cloned.1.call-done), kind=kOutput, calls=%fused_computation.52 | convolution fusion | flops 2416312320 | bytes 8650752 | tf_op jit(solution)/shard_map/dot_general | solution.py:137
  451.5 4.3 fusion.45
  455.8 5.4 all-reduce.1
  463.4 4.5 collective-permute-done.4
  470.3 5.3 all-reduce
  475.6 4.0 multiply_convert_fusion
  479.6 5.8 collective-permute-start.5
  488.3 5.7 convolution_convert_fusion
  494.0 7.7 %all-to-all-start = ((bf16[32,48,1536]{2,1,0:T(8,128)(2,1)}), bf16[32,48,1536]{2,1,0:T(8,128)(2,1)}, u32[]{:S(2)}, u32[]{:S(2)}) async-start(bf16[32,48,1536]{2,1,0:T(8,128)(2,1)} %bitcast.117), calls=%async_computation | async-start | bytes 9437184 | tf_op jit(solution)/shard_map/all_to_all | solution.py:194
  501.7 4.7 select_bitcast_fusion
  506.4 67.9 %all-to-all-done = bf16[32,48,1536]{2,1,0:T(8,128)(2,1)} async-done(((bf16[32,48,1536]{2,1,0:T(8,128)(2,1)}), bf16[32,48,1536]{2,1,0:T(8,128)(2,1)}, u32[]{:S(2)}, u32[]{:S(2)}) %all-to-all-start) | async-done | bytes 4718624 | tf_op jit(solution)/shard_map/all_to_all | solution.py:194
  574.3 3.7 convert_reduce_fusion
  (86 shorter events, 35.0 us)
Async XLA Ops:
  7.2 5.5 copy-start
  7.2 5.4 copy-start.16
  7.2 264.8 %all-gather.2.cloned.1.call-start = ((), (), s32[]{:S(2)}) async-start(), calls=%async_computation.1 | async-start | bytes 24330240 | tf_op jit(solution)/shard_map/all_gather | solution.py:90
  12.6 14.8 %copy-start.18 = (s32[2]{0:T(128)S(1)}, s32[2]{0:T(128)}, u32[]{:S(2)}) copy-start(s32[2]{0:T(128)} %param.17) | copy-start | bytes 28
  27.4 3.7 copy-start.17
  37.3 2.7 copy-start.2
  38.0 1.3 copy-start.14
  304.2 2.2 copy-start.9
  329.9 2.2 copy-start.4
  348.0 37.0 %collective-permute-start = (bf16[512,1536]{1,0:T(8,128)(2,1)S(1)}, bf16[512,1536]{1,0:T(8,128)(2,1)}, u32[]{:S(2)}, u32[]{:S(2)}) collective-permute-start(bf16[512,1536]{1,0:T(8,128)(2,1)S(1)} %convolution_convert_fusion.1), channel_id=1, source_target_pairs={{0,1},{1,0},{2,3},{3,2},{4,5},{5,4},{6,7},{7,6},{8,9},{9,8},{10,11... | collective-permute-start | bytes 4718600 | tf_op jit(solution)/shard_map/ppermute | solution.py:24
  386.8 4.9 copy-start.6
  393.5 1.1 copy-start.8
  393.5 35.9 %collective-permute-start.1 = (bf16[512,1536]{0,1:T(8,128)(2,1)S(1)}, bf16[512,1536]{0,1:T(8,128)(2,1)}, u32[]{:S(2)}, u32[]{:S(2)}) collective-permute-start(bf16[512,1536]{0,1:T(8,128)(2,1)S(1)} %copy.27), channel_id=1, source_target_pairs={{0,1},{1,0},{2,3},{3,2},{4,5},{5,4},{6,7},{7,6},{8,9},{9,8},{10,11... | collective-permute-start | bytes 4718600 | tf_op jit(solution)/shard_map/ppermute | solution.py:24
  432.6 9.0 %collective-permute-start.2 = (bf16[512,3072]{0,1:T(8,128)(2,1)S(1)}, bf16[512,3072]{0,1:T(8,128)(2,1)S(1)}, u32[]{:S(2)}, u32[]{:S(2)}) collective-permute-start(bf16[512,3072]{0,1:T(8,128)(2,1)S(1)} %maximum_select_fusion), channel_id=1, source_target_pairs={{0,2},{1,3},{4,6},{5,7},{8,10},{9,11},{12,14},{13,15},{16,18},{17,... | collective-permute-start | bytes 9437192 | tf_op jit(solution)/shard_map/ppermute | solution.py:14
  442.0 6.2 %copy-start.7 = (bf16[512,3072]{0,1:T(8,128)(2,1)}, bf16[512,3072]{0,1:T(8,128)(2,1)S(1)}, u32[]{:S(2)}) copy-start(bf16[512,3072]{0,1:T(8,128)(2,1)S(1)} %broadcast_select_fusion) | copy-start | bytes 9437188
  442.0 6.4 %copy-start.15 = (f32[2,2,3072]{2,1,0:T(2,128)S(1)}, f32[2,2,3072]{2,1,0:T(2,128)}, u32[]{:S(2)}) copy-start(f32[2,2,3072]{2,1,0:T(2,128)} %param.24) | copy-start | bytes 147460
  448.2 2.4 copy-start.10
  448.2 2.4 collective-permute-start.3
  450.6 0.9 copy-start.11
  455.8 19.8 %copy-start.3 = (f32[2,256,1536]{2,1,0:T(8,128)}, f32[2,256,1536]{2,1,0:T(8,128)S(1)}, u32[]{:S(2)}) copy-start(f32[2,256,1536]{2,1,0:T(8,128)S(1)} %get-tuple-element.8) | copy-start | bytes 9437188
  455.8 6.1 %copy-start.12 = (bf16[1536,64]{0,1:T(8,128)(2,1)S(1)}, bf16[1536,64]{0,1:T(8,128)(2,1)}, u32[]{:S(2)}) copy-start(bf16[1536,64]{0,1:T(8,128)(2,1)} %param.23) | copy-start | bytes 589828
  461.3 2.1 copy-start.13
  462.5 5.4 collective-permute-start.4
  468.6 1.7 copy-start.5
  479.6 8.7 %collective-permute-start.5 = (bf16[512,1536]{1,0:T(8,128)(2,1)}, bf16[512,1536]{1,0:T(8,128)(2,1)S(1)}, u32[]{:S(2)}, u32[]{:S(2)}) collective-permute-start(bf16[512,1536]{1,0:T(8,128)(2,1)} %bitcast.40), channel_id=1, source_target_pairs={{2,0},{3,1},{6,4},{7,5},{10,8},{11,9},{14,12},{15,13},{18,16},{19,... | collective-permute-start | bytes 4718600 | tf_op jit(solution)/shard_map/ppermute | solution.py:14
  494.0 80.3 %all-to-all-start = ((bf16[32,48,1536]{2,1,0:T(8,128)(2,1)}), bf16[32,48,1536]{2,1,0:T(8,128)(2,1)}, u32[]{:S(2)}, u32[]{:S(2)}) async-start(bf16[32,48,1536]{2,1,0:T(8,128)(2,1)} %bitcast.117), calls=%async_computation | async-start | bytes 9437184 | tf_op jit(solution)/shard_map/all_to_all | solution.py:194
  501.7 76.4 %copy-start.1 = (bf16[2,256,3072]{2,1,0:T(8,128)(2,1)S(1)}, bf16[2,256,3072]{2,1,0:T(8,128)(2,1)}, u32[]{:S(2)}) copy-start(bf16[2,256,3072]{2,1,0:T(8,128)(2,1)} %param.14) | copy-start | bytes 9437188
Sparse Core Ops, SparseCore 0:
  12.7 259.2 all-gather.1
where the time goes:
time: 595 us; the launch traced here: 585 us
  waiting for transfers between devices  380 us (64%)
  local copies, waits for them, and re-layouts  68.8 us (12%)
  matrix products  49.4 us (8%)
  other arithmetic  44.1 us (7%)
  starting transfers between devices  17.6 us (3%)
  between operations  14.7 us (2%)
  blocking collectives  10.7 us (2%)
    all_gather x1, waiting for transfers between devices, local(): gathered = lax.all_gather(packed, 'ctl', axis=0, tiled=True)  228 us
    ppermute x3, waiting for transfers between devices, swap(): return lax.ppermute(value, axis, [(0, 1), (1, 0)])  72.2 us
    all_to_all x1, waiting for transfers between devices, local(): received = lax.all_to_all(group_parts, 'ctl', 0, 0, tiled=True)  67.9 us
    dot_general x2, local copies, waits for them, and re-layouts, local(): jnp.dot(text_flat, pair_weight, preferred_element_type=jnp.float32)  20.7 us
    gather x1, local copies, waits for them, and re-layouts, local(): jnp.take(latent, order_row, axis=0)  14.8 us
  transfers between devices with their start and end apart: 8, of which 8 were waited for; matrix products, arithmetic and copies ran while one was open for 7% of the time, Pallas kernels for 0%

commit v1 on v0

--- a/solution.py
+++ b/solution.py
@@ -87,7 +87,12 @@
     packed = jnp.concatenate(
         [qkv_weight[0].reshape(local_rows, 3 * local_heads), out_weight[0].T, own_cols], axis=1
     )
-    gathered = lax.all_gather(packed, "ctl", axis=0, tiled=True)
+    views = []
+    for _ in range(lax.psum(1, axis_name="ctl")):
+        views.append(packed)
+    fresh = jnp.stack(views)
+    b_now = lax.all_to_all(fresh, axis_name="ctl", split_axis=0, concat_axis=0)
+    gathered = jnp.concatenate(b_now, 0)
     count_rows = gathered.shape[0]
     query_weight = gathered[:, :local_heads]
     pair_weight = gathered[:, local_heads : 3 * local_heads]

time: 595 us -> 768 us (1.29)
  the two profiles are of different devices: /device:TPU:113 before, /device:TPU:69 now
where the time goes in v1:
time: 768 us; the launch traced here: 757 us
  waiting for transfers between devices  492 us (64%)
  starting transfers between devices  84.8 us (11%)
  local copies, waits for them, and re-layouts  77.1 us (10%)
  matrix products  48 us (6%)
  other arithmetic  43.4 us (6%)
  blocking collectives  10.7 us (1%)
    all_to_all x1, waiting for transfers between devices, local(): b_now = lax.all_to_all(fresh, axis_name='ctl', split_axis=0, concat_axis=0)  336 us
    all_to_all x1, waiting for transfers between devices, local(): received = lax.all_to_all(group_parts, 'ctl', 0, 0, tiled=True)  72.5 us
    ppermute x3, waiting for transfers between devices, swap(): return lax.ppermute(value, axis, [(0, 1), (1, 0)])  71.5 us
    all_to_all x1, starting transfers between devices, local(): received = lax.all_to_all(group_parts, 'ctl', 0, 0, tiled=True)  68.2 us
    dot_general x2, local copies, waits for them, and re-layouts, local(): jnp.dot(text_flat, pair_weight, preferred_element_type=jnp.float32)  20.7 us
  transfers between devices with their start and end apart: 8, of which 8 were waited for; matrix products, arithmetic and copies ran while one was open for 5% of the time, Pallas kernels for 0%

profile of v1, /device:TPU:69, one launch (start us, length us, event | category | flops | bytes accessed | tf_op | source)
XLA Modules:
  0.0 757.4 jit_solution(1432896113467647215)
XLA Ops:
  5.1 8.1 %stack.2 = bf16[32,96,3840]{2,1,0:T(8,128)(2,1)} broadcast(bf16[96,3840]{1,0:T(8,128)(2,1)S(1)} %pad_maximum_fusion.1), dimensions={1,2} | broadcast | bytes 24330240 | tf_op jit(solution)/shard_map/stack | solution.py:93
  13.2 8.3 %all-to-all-start = ((bf16[32,96,3840]{2,1,0:T(8,128)(2,1)}), bf16[32,96,3840]{2,1,0:T(8,128)(2,1)}, u32[]{:S(2)}, u32[]{:S(2)}) async-start(bf16[32,96,3840]{2,1,0:T(8,128)(2,1)} %stack.2), calls=%async_computation | async-start | bytes 47185920 | tf_op jit(solution)/shard_map/all_to_all | solution.py:94
  21.6 14.8 %gather_fusion.1 = bf16[512,3072]{1,0:T(8,128)(2,1)} fusion(bf16[2,256,3072]{2,1,0:T(8,128)(2,1)S(1)} %copy-done, s32[512]{0:T(512)S(1)} %bitcast.110), kind=kCustom, calls=%fused_computation.1 | custom fusion | bytes 6295552 | tf_op jit(solution)/shard_map/vmap(jit(_take))/gather | solution.py:72
  36.3 3.7 gather_fusion
  41.7 4.4 multiply_add_fusion
  48.7 3.6 add_convert_fusion
  52.3 336.1 %all-to-all-done = bf16[32,96,3840]{2,1,0:T(8,128)(2,1)} async-done(((bf16[32,96,3840]{2,1,0:T(8,128)(2,1)}), bf16[32,96,3840]{2,1,0:T(8,128)(2,1)}, u32[]{:S(2)}, u32[]{:S(2)}) %all-to-all-start) | async-done | bytes 23592992 | tf_op jit(solution)/shard_map/all_to_all | solution.py:94
  388.4 8.0 %slice_bitcast_fusion = bf16[1536,3072]{0,1:T(8,128)(2,1)} fusion(bf16[3072,3840]{1,0:T(8,128)(2,1)} %bitcast.10), kind=kLoop, calls=%fused_computation.3 | loop fusion | bytes 18874368 | tf_op jit(solution)/shard_map/dot_general | solution.py:102
  396.4 7.9 %fusion.46 = (bf16[3072,768]{1,0:T(8,128)(2,1)}, bf16[768,3072]{0,1:T(8,128)(2,1)}) fusion(bf16[3072,3840]{1,0:T(8,128)(2,1)} %bitcast.10), kind=kLoop, calls=%fused_computation.99 | loop fusion | bytes 18874368 | tf_op jit(solution)/shard_map/slice | solution.py:99
  404.4 12.6 %copy.21 = bf16[1536,3072]{1,0:T(8,128)(2,1)} copy(bf16[1536,3072]{0,1:T(8,128)(2,1)} %slice_bitcast_fusion) | data formatting | bytes 18874368 | tf_op jit(solution)/shard_map/dot_general | solution.py:102
  417.0 11.5 %fusion.4 = f32[2,384,2,6,128]{1,4,3,2,0:T(8,128)S(1)} fusion(bf16[2,6,128,3072,1]{3,2,1,0,4:T(8,128)(2,1)} %bitcast.114, bf16[2,384,3072]{2,1,0:T(8,128)(2,1)} %add_convert_fusion), kind=kOutput, calls=%fused_computation.14 | convolution fusion | flops 7247757312 | bytes 18874368 | tf_op jit(solution)/shard_map/dot_general | solution.py:102
  431.0 6.7 copy.22
  437.7 6.2 multiply_reduce_fusion.5
  448.7 10.0 %fusion.21 = bf16[2,256,6,128]{1,3,2,0:T(8,128)(2,1)S(1)} fusion(f32[2,6,256]{2,1,0:T(8,128)S(1)} %fusion.48, f32[2,384,2,6,128]{1,4,3,2,0:T(8,128)} %copy-done.9, f32[2,6,256,384]{3,2,1,0:T(8,128)} %copy-done.4), kind=kOutput, calls=%fused_computation.53 | convolution fusion | flops 308284800 | bytes 11415552 | tf_op jit(solution)/shard_map/bhij,bjhd->bihd/dot_general | solution.py:114
  459.7 3.1 convolution_convert_fusion.1
  466.3 32.6 %collective-permute-done = bf16[512,1536]{1,0:T(8,128)(2,1)} collective-permute-done((bf16[512,1536]{1,0:T(8,128)(2,1)S(1)}, bf16[512,1536]{1,0:T(8,128)(2,1)}, u32[]{:S(2)}, u32[]{:S(2)}) %collective-permute-start) | collective-permute-done | bytes 1572896 | tf_op jit(solution)/shard_map/ppermute | solution.py:24
  500.8 4.9 fusion.27
  508.5 33.9 %collective-permute-done.1 = bf16[512,1536]{0,1:T(8,128)(2,1)} collective-permute-done((bf16[512,1536]{0,1:T(8,128)(2,1)S(1)}, bf16[512,1536]{0,1:T(8,128)(2,1)}, u32[]{:S(2)}, u32[]{:S(2)}) %collective-permute-start.1) | collective-permute-done | bytes 1572896 | tf_op jit(solution)/shard_map/ppermute | solution.py:24
  542.4 3.3 maximum_select_fusion
  547.1 8.6 %collective-permute-done.2 = bf16[512,3072]{0,1:T(8,128)(2,1)S(1)} collective-permute-done((bf16[512,3072]{0,1:T(8,128)(2,1)S(1)}, bf16[512,3072]{0,1:T(8,128)(2,1)S(1)}, u32[]{:S(2)}, u32[]{:S(2)}) %collective-permute-start.2) | collective-permute-done | bytes 3145760 | tf_op jit(solution)/shard_map/ppermute | solution.py:14
  556.1 6.1 fusion.18
  565.5 4.4 fusion.45
  569.9 5.4 all-reduce.1
  577.1 4.9 collective-permute-done.4
  584.4 5.3 all-reduce
  589.7 4.0 multiply_convert_fusion
  593.7 5.8 collective-permute-start.5
  602.4 5.7 convolution_convert_fusion
  608.1 68.2 %all-to-all-start.1 = ((bf16[32,48,1536]{2,1,0:T(8,128)(2,1)}), bf16[32,48,1536]{2,1,0:T(8,128)(2,1)}, u32[]{:S(2)}, u32[]{:S(2)}) async-start(bf16[32,48,1536]{2,1,0:T(8,128)(2,1)} %bitcast.118), calls=%async_computation.1 | async-start | bytes 9437184 | tf_op jit(solution)/shard_map/all_to_all | solution.py:199
  676.3 4.7 select_bitcast_fusion
  680.9 72.5 %all-to-all-done.1 = bf16[32,48,1536]{2,1,0:T(8,128)(2,1)} async-done(((bf16[32,48,1536]{2,1,0:T(8,128)(2,1)}), bf16[32,48,1536]{2,1,0:T(8,128)(2,1)}, u32[]{:S(2)}, u32[]{:S(2)}) %all-to-all-start.1) | async-done | bytes 4718624 | tf_op jit(solution)/shard_map/all_to_all | solution.py:199
  753.4 3.7 convert_reduce_fusion
  (88 shorter events, 37.0 us)
Async XLA Ops:
  0.6 20.9 %copy-start = (bf16[2,256,3072]{2,1,0:T(8,128)(2,1)S(1)}, bf16[2,256,3072]{2,1,0:T(8,128)(2,1)}, u32[]{:S(2)}) copy-start(bf16[2,256,3072]{2,1,0:T(8,128)(2,1)} %param.14) | copy-start | bytes 9437188
  13.2 8.3 %copy-start.17 = (s32[2,256]{1,0:T(2,128)S(1)}, s32[2,256]{1,0:T(2,128)}, u32[]{:S(2)}) copy-start(s32[2,256]{1,0:T(2,128)} %param.15) | copy-start | bytes 6148
  13.2 375.2 %all-to-all-start = ((bf16[32,96,3840]{2,1,0:T(8,128)(2,1)}), bf16[32,96,3840]{2,1,0:T(8,128)(2,1)}, u32[]{:S(2)}, u32[]{:S(2)}) async-start(bf16[32,96,3840]{2,1,0:T(8,128)(2,1)} %stack.2), calls=%async_computation | async-start | bytes 47185920 | tf_op jit(solution)/shard_map/all_to_all | solution.py:94
  21.5 14.8 %copy-start.19 = (s32[2]{0:T(128)S(1)}, s32[2]{0:T(128)}, u32[]{:S(2)}) copy-start(s32[2]{0:T(128)} %param.17) | copy-start | bytes 28
  36.3 3.7 copy-start.18
  46.1 2.6 copy-start.2
  46.8 1.3 copy-start.15
  428.5 2.2 copy-start.9
  437.7 6.2 copy-start.10
  444.8 2.2 copy-start.4
  462.8 36.0 %collective-permute-start = (bf16[512,1536]{1,0:T(8,128)(2,1)S(1)}, bf16[512,1536]{1,0:T(8,128)(2,1)}, u32[]{:S(2)}, u32[]{:S(2)}) collective-permute-start(bf16[512,1536]{1,0:T(8,128)(2,1)S(1)} %convolution_convert_fusion.1), channel_id=1, source_target_pairs={{0,1},{1,0},{2,3},{3,2},{4,5},{5,4},{6,7},{7,6},{8,9},{9,8},{10,11... | collective-permute-start | bytes 4718600 | tf_op jit(solution)/shard_map/ppermute | solution.py:24
  500.7 4.9 copy-start.6
  507.4 1.1 copy-start.8
  507.4 35.0 %collective-permute-start.1 = (bf16[512,1536]{0,1:T(8,128)(2,1)S(1)}, bf16[512,1536]{0,1:T(8,128)(2,1)}, u32[]{:S(2)}, u32[]{:S(2)}) collective-permute-start(bf16[512,1536]{0,1:T(8,128)(2,1)S(1)} %copy.27), channel_id=1, source_target_pairs={{0,1},{1,0},{2,3},{3,2},{4,5},{5,4},{6,7},{7,6},{8,9},{9,8},{10,11... | collective-permute-start | bytes 4718600 | tf_op jit(solution)/shard_map/ppermute | solution.py:24
  545.8 9.9 %collective-permute-start.2 = (bf16[512,3072]{0,1:T(8,128)(2,1)S(1)}, bf16[512,3072]{0,1:T(8,128)(2,1)S(1)}, u32[]{:S(2)}, u32[]{:S(2)}) collective-permute-start(bf16[512,3072]{0,1:T(8,128)(2,1)S(1)} %maximum_select_fusion), channel_id=1, source_target_pairs={{0,2},{1,3},{4,6},{5,7},{8,10},{9,11},{12,14},{13,15},{16,18},{17,... | collective-permute-start | bytes 9437192 | tf_op jit(solution)/shard_map/ppermute | solution.py:14
  556.1 6.2 copy-start.7
  556.1 6.4 copy-start.16
  562.3 2.4 copy-start.11
  562.3 2.4 collective-permute-start.3
  564.6 0.9 copy-start.12
  569.9 19.8 %copy-start.3 = (f32[2,256,1536]{2,1,0:T(8,128)}, f32[2,256,1536]{2,1,0:T(8,128)S(1)}, u32[]{:S(2)}) copy-start(f32[2,256,1536]{2,1,0:T(8,128)S(1)} %get-tuple-element.8) | copy-start | bytes 9437188
  569.9 6.1 copy-start.13
  575.4 1.7 copy-start.14
  576.6 5.4 collective-permute-start.4
  582.7 1.7 copy-start.5
  593.7 8.7 %collective-permute-start.5 = (bf16[512,1536]{1,0:T(8,128)(2,1)}, bf16[512,1536]{1,0:T(8,128)(2,1)S(1)}, u32[]{:S(2)}, u32[]{:S(2)}) collective-permute-start(bf16[512,1536]{1,0:T(8,128)(2,1)} %bitcast.41), channel_id=1, source_target_pairs={{2,0},{3,1},{6,4},{7,5},{10,8},{11,9},{14,12},{15,13},{18,16},{19,... | collective-permute-start | bytes 4718600 | tf_op jit(solution)/shard_map/ppermute | solution.py:14
  608.1 145.4 %all-to-all-start.1 = ((bf16[32,48,1536]{2,1,0:T(8,128)(2,1)}), bf16[32,48,1536]{2,1,0:T(8,128)(2,1)}, u32[]{:S(2)}, u32[]{:S(2)}) async-start(bf16[32,48,1536]{2,1,0:T(8,128)(2,1)} %bitcast.118), calls=%async_computation.1 | async-start | bytes 9437184 | tf_op jit(solution)/shard_map/all_to_all | solution.py:199
  676.2 81.0 %copy-start.1 = (bf16[2,256,3072]{2,1,0:T(8,128)(2,1)S(1)}, bf16[2,256,3072]{2,1,0:T(8,128)(2,1)}, u32[]{:S(2)}) copy-start(bf16[2,256,3072]{2,1,0:T(8,128)(2,1)} %param.14) | copy-start | bytes 9437188
